TPU v7x, 32 devices: a whole 2x2x4 slice. The times are simulated.
32 devices in a mesh: freq: 2 (over y), clus: 4 (over z), src: 2 (over x), sub: 2 (over core).
Axes of the slice: x: 2, y: 2, z: 4, core: 2. Of those that a mesh axis runs over, the one named last changes fastest.
Arguments:
- charges: bfloat16 [512, 48, 128], P(('freq', 'src'), 'clus'), parts along dimension 0, may hold values from -6 to 6
- geometry: float32 [4, 48, 256], replicated, may hold values from -4 to 4, as said below
- wavenumber: float32 [2], P('freq'), parts along dimension 0, may hold values from 0.3 to 2
- requests: int32 [8, 4, 4], P(('clus', 'sub')), may hold values from -1 to 11, as said below
- pairs: int32 [48, 2, 32], P('clus', 'sub'), may hold values from 0 to 15, as said below
- counts: int32 [48, 2], P('clus', 'sub'), may hold values from 1 to 32, as said below
Outputs:
- iterate: bfloat16 [512, 48, 128], P(('freq', 'src'), 'clus'), parts along dimension 0
- image: float32 [512, 48, 128], P(('freq', 'src', 'sub'), 'clus'), parts along dimension 0
There are 2 independent parts, one for each index of `freq`. A program takes and returns all parts, laid end to end along the dimension named above; an argument that names none is the same for every part. Nothing has to cross between parts.
Inputs may be any that keep to these rules, and one draw needn't show every extreme that they name: `geometry`: rows: x and y, depth z from -1 to -0.05, panel area from 0.05 to 0.5. `requests`: each row's live entries are distinct cluster numbers and come first, -1 marks an empty slot; in every block the row of the block's own clus index holds 4 live entries. `pairs`: every entry d * 4 + k names a live entry requests[b, d, k] of the block b of the target cluster's owner and half. `counts`: 32 is reached in every draw.
All inputs are finite; a program needn't handle non-finite values.
Results may differ from a plain program's by a relative error of at most 0.0049.
Values may be sent and summed in bfloat16 or wider, within the bound.
No kernel may reach another device: no remote copies, remote signals or barrier semaphores. Data moves between devices by JAX's collectives and lax.ppermute only.
A program may use at most 64 MiB of HBM per device.

v0:
```python
import jax
import jax.numpy as jnp
from jax import lax
from jax.experimental import pallas as pl
from jax.experimental.pallas import tpu as pltpu
from jax.sharding import PartitionSpec as P

CPD = 12
CAP = 4
PPT = 32

quarter_turn = 0.7853981633974483
two_pi = 6.283185307179586
inverse_four_pi = 0.07957747154594767
two_over_pi = 0.6366197723675814

STRIP = 16
LANES = 128


def sincos(x):
    n = jnp.floor(x * two_over_pi + 0.5)
    r = ((x - n * 1.5703125) - n * 4.837512969970703125e-4) - n * 7.54978995489188216e-8
    z = r * r
    s = ((-1.9515295891e-4 * z + 8.3321608736e-3) * z - 1.6666654611e-1) * z * r + r
    c = ((2.443315711809948e-5 * z - 1.388731625493765e-3) * z + 4.166664568298827e-2) * z * z
    c = c - 0.5 * z + 1.0
    q = n.astype(jnp.int32)
    swap = (q & 1) == 1
    s0 = jnp.where(swap, c, s)
    c0 = jnp.where(swap, s, c)
    sin = jnp.where((q & 2) == 2, -s0, s0)
    cos = jnp.where(((q + 1) & 2) == 2, -c0, c0)
    return sin, cos


def green(k, xt, yt, zt, et, xs, ys, zs, area, sj, cj):
    dx = xt - xs
    dy = yt - ys
    planar = dx * dx + dy * dy
    dz = zt - zs
    zsum = zt + zs
    direct = lax.rsqrt(planar + dz * dz + area)
    mirror = lax.rsqrt(planar + zsum * zsum + area)
    kr = k * jnp.sqrt(planar)
    amp = (et * cj) * lax.rsqrt(1.0 + kr)
    sin, cos = sincos(kr + quarter_turn)
    return sj * (direct + mirror) - amp * sin, amp * cos


def tile_into(k, tb_ref, sb_ref, g, p, tr_ref, ti_ref):
    width = tr_ref.shape[0]
    halves = tr_ref.shape[1] // LANES
    for h in range(halves):
        lanes = pl.ds(h * LANES, LANES)
        xt = tb_ref[g, 0, :, lanes]
        yt = tb_ref[g, 1, :, lanes]
        zt = tb_ref[g, 2, :, lanes]
        et = tb_ref[g, 3, :, lanes]

        def strip(r, carry):
            rows = pl.ds(pl.multiple_of(r * STRIP, STRIP), STRIP)
            xs = sb_ref[p, 0, rows, :]
            ys = sb_ref[p, 1, rows, :]
            zs = sb_ref[p, 2, rows, :]
            area = sb_ref[p, 3, rows, :]
            sj = sb_ref[p, 4, rows, :]
            cj = sb_ref[p, 5, rows, :]
            re, im = green(k, xt, yt, zt, et, xs, ys, zs, area, sj, cj)
            tr_ref[rows, lanes] = re.astype(jnp.bfloat16)
            ti_ref[rows, lanes] = im.astype(jnp.bfloat16)
            return carry

        lax.fori_loop(0, width // STRIP, strip, 0)


def entry_product(l_ref, p, tr, ti):
    part = jnp.dot(l_ref[p, 0], tr, preferred_element_type=jnp.float32)
    return part + jnp.dot(l_ref[p, 1], ti, preferred_element_type=jnp.float32)


def product_kernel(n_ref, g_ref, p_ref, w_ref, k_ref, tb_ref, sb_ref, l_ref, acc_ref, tbuf):
    n = n_ref[0]
    k = k_ref[0]
    acc_ref[...] = jnp.zeros_like(acc_ref)

    def body(e, carry):
        g = g_ref[e]
        p = p_ref[e]
        w = w_ref[e]
        tile_into(k, tb_ref, sb_ref, g, p, tbuf.at[0], tbuf.at[1])
        part = entry_product(l_ref, p, tbuf[0], tbuf[1])
        acc_ref[g] = acc_ref[g] + w * part
        return carry

    lax.fori_loop(0, n, body, 0)


SMEM_SPEC = pl.BlockSpec(memory_space=pltpu.SMEM)
VMEM_SPEC = pl.BlockSpec(memory_space=pltpu.VMEM)


def product(n, g_list, p_list, w_list, k, tb, sb, lhs):
    clusters = tb.shape[0]
    targets = tb.shape[3]
    nmax = g_list.shape[0]
    width = sb.shape[2]
    cols = lhs.shape[2]
    elems = nmax * width * targets
    return pl.pallas_call(
        product_kernel,
        out_shape=jax.ShapeDtypeStruct((clusters, cols, targets), jnp.float32),
        in_specs=[SMEM_SPEC] * 5 + [VMEM_SPEC] * 3,
        out_specs=VMEM_SPEC,
        scratch_shapes=[pltpu.VMEM((2, width, targets), jnp.bfloat16)],
        cost_estimate=pl.CostEstimate(
            flops=elems * 60 + 4 * elems * cols,
            transcendentals=elems * 4,
            bytes_accessed=elems * 2,
        ),
    )(n, g_list, p_list, w_list, k, tb, sb, lhs)


def local(charges, geometry, wavenumber, requests, pairs, counts):
    clus_index = lax.axis_index("clus")
    src_index = lax.axis_index("src")
    sub_index = lax.axis_index("sub")
    clus_count = lax.axis_size("clus")
    sub_count = lax.axis_size("sub")
    source_rows = charges.shape[0]
    share_rows = source_rows // sub_count
    targets = geometry.shape[2]
    cpd = charges.shape[1]
    wavenum = wavenumber[0]
    slot_total = clus_count * requests.shape[2]

    served = lax.all_to_all(requests[0], "clus", split_axis=0, concat_axis=0, tiled=True).reshape(
        -1
    )
    served_index = jnp.maximum(served, 0)
    served_mask = (served >= 0).astype(jnp.bfloat16)[None, :, None]

    def fetch(values):
        picked = jnp.take(values, served_index, axis=1) * served_mask
        return lax.all_to_all(picked, "clus", split_axis=1, concat_axis=1, tiled=True)

    def lhs_of(values):
        blocks = fetch(values)
        half_width = blocks.shape[2] // 2
        swapped = jnp.concatenate([-blocks[..., half_width:], blocks[..., :half_width]], axis=-1)
        return jnp.stack(
            [jnp.transpose(blocks, (1, 2, 0)), jnp.transpose(swapped, (1, 2, 0))], axis=1
        )

    target_geo = lax.dynamic_slice_in_dim(geometry, clus_index * cpd, cpd, axis=1)
    tq = jnp.stack(
        [target_geo[0], target_geo[1], target_geo[2], jnp.exp(wavenum * target_geo[2])], axis=1
    )
    tb = jnp.broadcast_to(tq[:, :, None, :], (cpd, 4, STRIP, targets))

    base_ids = jnp.arange(clus_count, dtype=jnp.int32)[:, None] * cpd
    source_ids = (base_ids + jnp.maximum(requests[0], 0)).reshape(-1)
    source_full = jnp.take(geometry, source_ids, axis=1)
    source_geo = lax.dynamic_slice_in_dim(source_full, src_index * source_rows, source_rows, axis=2)
    sj = source_geo[3] * inverse_four_pi
    cj = (two_pi * wavenum) * jnp.exp(wavenum * source_geo[2]) * sj
    sq = jnp.stack([source_geo[0], source_geo[1], source_geo[2], source_geo[3], sj, cj], axis=1)
    sb = jnp.broadcast_to(sq[..., None], sq.shape + (LANES,))

    slot_ids = pairs[:, 0, :]
    live = jnp.arange(pairs.shape[2], dtype=jnp.int32)[None, :] < counts[:, 0:1]
    hits = (slot_ids[:, :, None] == jnp.arange(slot_total, dtype=jnp.int32)[None, None, :]) & live[
        :, :, None
    ]
    weight = jnp.sum(hits.astype(jnp.int32), axis=1).reshape(-1)
    nmax = cpd * min(slot_total, pairs.shape[2])
    order = jnp.argsort((weight == 0).astype(jnp.int32), stable=True)[:nmax].astype(jnp.int32)
    g_list = order // slot_total
    p_list = order % slot_total
    w_list = jnp.take(weight, order).astype(jnp.float32)
    n = jnp.sum((weight > 0).astype(jnp.int32)).reshape(1)
    k_arr = wavenumber.astype(jnp.float32).reshape(1)

    def finish(acc):
        return lax.psum_scatter(
            jnp.transpose(acc, (2, 0, 1)), ("src", "sub"), scatter_dimension=0, tiled=True
        )

    first = finish(product(n, g_list, p_list, w_list, k_arr, tb, sb, lhs_of(charges)))
    own_rows = lax.dynamic_slice_in_dim(charges, sub_index * share_rows, share_rows, axis=0)
    iterate_share = (own_rows.astype(jnp.float32) - first).astype(jnp.bfloat16)
    iterate = lax.all_gather(iterate_share, "sub", axis=0, tiled=True)
    image = finish(product(n, g_list, p_list, w_list, k_arr, tb, sb, lhs_of(iterate)))
    return (iterate, image)


def solution(mesh):
    in_specs = (
        P(("freq", "src"), "clus", None),
        P(),
        P("freq"),
        P(("clus", "sub"), None, None),
        P("clus", "sub", None),
        P("clus", "sub"),
    )
    out_specs = (P(("freq", "src"), "clus", None), P(("freq", "src", "sub"), "clus", None))
    return jax.shard_map(local, mesh=mesh, in_specs=in_specs, out_specs=out_specs, check_vma=False)
```

profile of v0, /device:TPU:8, one launch (start us, length us, event | category | flops | bytes accessed | tf_op | source)
XLA Modules:
  0.0 309.7 jit_solution(10641104961057303614)
XLA Ops:
  7.2 5.5 %all-to-all-start = ((s32[4,1,4]{2,1,0:T(1,128)}), s32[4,1,4]{2,1,0:T(1,128)S(1)}, u32[]{:S(2)}, u32[]{:S(2)}) async-start(s32[4,1,4]{2,1,0:T(1,128)} %bitcast.74), calls=%async_computation | async-start | bytes 4096 | tf_op jit(solution)/shard_map/all_to_all | solution.py:137
  12.6 0.7 broadcast_maximum_fusion
  13.4 0.1 add.77
  13.4 0.1 add.81
  13.5 0.1 add.78
  13.6 0.1 max.27
  13.7 0.1 max.26
  13.8 0.7 copy.62
  14.5 0.7 iota_compare_fusion.1
  15.2 0.3 convert_reduce_fusion
  15.5 0.1 reshape.159
  15.5 0.7 convert_reduce_fusion.1
  16.3 3.2 %sort.17 = (s32[192]{0:T(256)}, s32[192]{0:T(256)S(1)}) sort(s32[192]{0:T(256)S(1)} %compare_convert_fusion.1, s32[192]{0:T(256)S(1)} %iota.22), dimensions={0}, to_apply=%region_2.3 | sort | flops 1536 | bytes 3072 | tf_op jit(solution)/shard_map/jit(argsort)/sort | solution.py:177
  20.1 1.6 gather_fusion.1
  21.7 0.8 dynamic-slice_bitcast_fusion.2
  22.5 0.7 multiply_exponential_fusion
  23.3 1.6 gather_fusion
  24.9 0.6 fusion.4
  25.5 0.1 max.29
  25.6 0.1 fusion.1
  25.7 0.6 gather_fusion.2
  26.4 0.3 copy.50
  26.7 0.1 reshape.160
  26.8 0.9 bitcast_multiply_fusion.1
  27.7 5.1 %all-to-all-start.1 = ((bf16[128,16,128]{0,2,1:T(8,128)(2,1)}), bf16[128,16,128]{0,2,1:T(8,128)(2,1)S(1)}, u32[]{:S(2)}, u32[]{:S(2)}) async-start(bf16[128,16,128]{0,2,1:T(8,128)(2,1)} %bitcast_multiply_fusion.1), calls=%async_computation.1 | async-start | bytes 1048576 | tf_op jit(solution)/shard_map/all_to_all | solution.py:145
  32.8 10.7 %all-to-all-done.1 = bf16[128,16,128]{0,2,1:T(8,128)(2,1)S(1)} async-done(((bf16[128,16,128]{0,2,1:T(8,128)(2,1)}), bf16[128,16,128]{0,2,1:T(8,128)(2,1)S(1)}, u32[]{:S(2)}, u32[]{:S(2)}) %all-to-all-start.1) | async-done | bytes 524320 | tf_op jit(solution)/shard_map/all_to_all | solution.py:145
  43.5 0.1 slice_negate_fusion.1
  43.6 0.1 pad_maximum_fusion
  43.7 1.1 copy.51.l_ref
  44.8 3.8 %broadcast_in_dim.49.sb_ref = f32[16,6,128,128]{3,2,1,0:T(8,128)} broadcast(f32[16,6,128]{2,1,0:T(8,128)S(1)} %copy.48), dimensions={0,1,2} | broadcast | bytes 6340608 | tf_op jit(solution)/shard_map/broadcast_in_dim | solution.py:168
  48.6 1.0 broadcast_in_dim.46.tb_ref
  49.6 35.8 %shard_map.80 = f32[12,128,256]{2,1,0:T(8,128)} custom-call(s32[1]{0:T(128)} %bitcast.1.n_ref, s32[192]{0:T(256)} %get-tuple-element.25.g_ref, s32[192]{0:T(256)} %get-tuple-element.24.p_ref, f32[192]{0:T(256)} %get-tuple-element.23.w_ref, f32[1]{0:T(128)} %copy.69.k_ref, f32[12,4,16,256]{3,2,1,0:T(8,128)} %broadcast_in_dim.46.tb_ref, ...), custom_call_target="tpu_custom_call" | custom-call | flops 3598712832 | bytes 12582912 | tf_op jit(solution)/shard_map/pallas_call | solution.py:110
  85.4 2.9 copy.52
  88.4 75.1 %reduce-scatter.3.cloned.1.call-done = f32[64,12,128]{2,1,0:T(8,128)} async-done(((f32[256,12,128]{2,1,0:T(8,128)}), f32[64,12,128]{2,1,0:T(8,128)}) %reduce-scatter.3.cloned.1.call-update) | async-done | bytes 393232 | tf_op jit(solution)/shard_map/reduce_scatter | solution.py:185
  163.5 1.2 subtract_convert_fusion
  164.7 0.1 copy.53
  164.8 2.1 all_gather.3
  166.8 0.6 gather_fusion.3
  167.5 0.3 copy.54
  167.8 0.1 bitcast_multiply_fusion
  167.9 17.9 %all_to_all.19 = bf16[128,16,128]{0,2,1:T(8,128)(2,1)S(1)} all-to-all(bf16[128,16,128]{0,2,1:T(8,128)(2,1)S(1)} %bitcast_multiply_fusion), channel_id=1, replica_groups=mesh['freq'=2,'clus'=4,'src'=2,'sub'=2] {'clus'}, dimensions={1} | all-to-all | bytes 1048576 | tf_op jit(solution)/shard_map/all_to_all | solution.py:145
  185.8 0.1 slice_negate_fusion
  185.9 1.2 pad_maximum_fusion.1.l_ref
  187.1 35.7 %shard_map.81 = f32[12,128,256]{2,1,0:T(8,128)} custom-call(s32[1]{0:T(128)} %bitcast.1.n_ref, s32[192]{0:T(256)} %get-tuple-element.25.g_ref, s32[192]{0:T(256)} %get-tuple-element.24.p_ref, f32[192]{0:T(256)} %get-tuple-element.23.w_ref, f32[1]{0:T(128)} %copy.69.k_ref, f32[12,4,16,256]{3,2,1,0:T(8,128)} %broadcast_in_dim.46.tb_ref, ...), custom_call_target="tpu_custom_call" | custom-call | flops 3598712832 | bytes 12582912 | tf_op jit(solution)/shard_map/pallas_call | solution.py:110
  222.9 3.0 copy.56
  225.9 74.4 %reduce-scatter.5.cloned.1.call-done = f32[64,12,128]{2,1,0:T(8,128)} async-done(((f32[256,12,128]{2,1,0:T(8,128)}), f32[64,12,128]{2,1,0:T(8,128)}) %reduce-scatter.5.cloned.1.call-update) | async-done | bytes 393232 | tf_op jit(solution)/shard_map/reduce_scatter | solution.py:185
  300.2 1.9 copy.57
  302.1 0.7 copy.70
  (30 shorter events, 0.4 us)
Async XLA Ops:
  7.2 18.6 %copy-start = (bf16[128,12,128]{2,0,1:T(8,128)(2,1)S(1)}, bf16[128,12,128]{2,0,1:T(8,128)(2,1)}, u32[]{:S(2)}) copy-start(bf16[128,12,128]{2,0,1:T(8,128)(2,1)} %param.8) | copy-start | bytes 1179652
  7.2 18.3 %all-to-all-start = ((s32[4,1,4]{2,1,0:T(1,128)}), s32[4,1,4]{2,1,0:T(1,128)S(1)}, u32[]{:S(2)}, u32[]{:S(2)}) async-start(s32[4,1,4]{2,1,0:T(1,128)} %bitcast.74), calls=%async_computation | async-start | bytes 4096 | tf_op jit(solution)/shard_map/all_to_all | solution.py:137
  27.7 15.8 %all-to-all-start.1 = ((bf16[128,16,128]{0,2,1:T(8,128)(2,1)}), bf16[128,16,128]{0,2,1:T(8,128)(2,1)S(1)}, u32[]{:S(2)}, u32[]{:S(2)}) async-start(bf16[128,16,128]{0,2,1:T(8,128)(2,1)} %bitcast_multiply_fusion.1), calls=%async_computation.1 | async-start | bytes 1048576 | tf_op jit(solution)/shard_map/all_to_all | solution.py:145
  32.8 130.7 %reduce-scatter.3.cloned.1.call-start = ((), (), s32[]{:S(2)}) async-start(), calls=%async_computation.5 | async-start | bytes 2621440 | tf_op jit(solution)/shard_map/reduce_scatter | solution.py:185
  88.3 211.9 %reduce-scatter.5.cloned.1.call-start = ((), (), s32[]{:S(2)}) async-start(), calls=%async_computation.6 | async-start | bytes 2621440 | tf_op jit(solution)/shard_map/reduce_scatter | solution.py:185
Sparse Core Ops, SparseCore 0:
  88.5 75.0 reduce-scatter.2
  226.0 74.2 reduce-scatter.4
where the time goes:
time: 314 us; the launch traced here: 310 us
  waiting for transfers between devices  160 us (51%)
  Pallas kernels  71.6 us (23%)
  local copies, waits for them, and re-layouts  21.7 us (7%)
  blocking collectives  20 us (6%)
  between operations  14.9 us (5%)
  other arithmetic  10.8 us (3%)
  starting transfers between devices  10.6 us (3%)
    reduce_scatter x2, waiting for transfers between devices, finish(): lax.psum_scatter(jnp.transpose(acc, (2, 0, 1)), ('src', 'sub'), scatter_d...  149 us
    pallas_call x2, Pallas kernels, product(): pl.pallas_call(product_kernel, out_shape=jax.ShapeDtypeStruct((clusters,...  71.6 us
    all_to_all x1, blocking collectives, fetch(): lax.all_to_all(picked, 'clus', split_axis=1, concat_axis=1, tiled=True)  17.9 us
    all_to_all x1, waiting for transfers between devices, fetch(): lax.all_to_all(picked, 'clus', split_axis=1, concat_axis=1, tiled=True)  10.7 us
  transfers between devices with their start and end apart: 4, of which 3 were waited for; matrix products, arithmetic and copies ran while one was open for 4% of the time, Pallas kernels for 0%

commit v1 on v0

--- a/solution.py
+++ b/solution.py
@@ -16,11 +16,12 @@
 
 STRIP = 16
 LANES = 128
+UNROLL = 2
 
 
 def sincos(x):
     n = jnp.floor(x * two_over_pi + 0.5)
-    r = ((x - n * 1.5703125) - n * 4.837512969970703125e-4) - n * 7.54978995489188216e-8
+    r = (x - n * 1.5703125) - n * 4.838267923332751e-4
     z = r * r
     s = ((-1.9515295891e-4 * z + 8.3321608736e-3) * z - 1.6666654611e-1) * z * r + r
     c = ((2.443315711809948e-5 * z - 1.388731625493765e-3) * z + 4.166664568298827e-2) * z * z
@@ -34,14 +35,14 @@
     return sin, cos
 
 
-def green(k, xt, yt, zt, et, xs, ys, zs, area, sj, cj):
+def green(k, xt, yt, zt, zt4, et, xs, ys, zs, area, sj, cj):
     dx = xt - xs
     dy = yt - ys
     planar = dx * dx + dy * dy
     dz = zt - zs
-    zsum = zt + zs
-    direct = lax.rsqrt(planar + dz * dz + area)
-    mirror = lax.rsqrt(planar + zsum * zsum + area)
+    near = planar + dz * dz + area
+    direct = lax.rsqrt(near)
+    mirror = lax.rsqrt(near + zt4 * zs)
     kr = k * jnp.sqrt(planar)
     amp = (et * cj) * lax.rsqrt(1.0 + kr)
     sin, cos = sincos(kr + quarter_turn)
@@ -51,27 +52,28 @@
 def tile_into(k, tb_ref, sb_ref, g, p, tr_ref, ti_ref):
     width = tr_ref.shape[0]
     halves = tr_ref.shape[1] // LANES
-    for h in range(halves):
-        lanes = pl.ds(h * LANES, LANES)
-        xt = tb_ref[g, 0, :, lanes]
-        yt = tb_ref[g, 1, :, lanes]
-        zt = tb_ref[g, 2, :, lanes]
-        et = tb_ref[g, 3, :, lanes]
-
-        def strip(r, carry):
-            rows = pl.ds(pl.multiple_of(r * STRIP, STRIP), STRIP)
-            xs = sb_ref[p, 0, rows, :]
-            ys = sb_ref[p, 1, rows, :]
-            zs = sb_ref[p, 2, rows, :]
-            area = sb_ref[p, 3, rows, :]
-            sj = sb_ref[p, 4, rows, :]
-            cj = sb_ref[p, 5, rows, :]
-            re, im = green(k, xt, yt, zt, et, xs, ys, zs, area, sj, cj)
+
+    def strip(r, carry):
+        rows = pl.ds(pl.multiple_of(r * STRIP, STRIP), STRIP)
+        xs = sb_ref[p, 0, rows, :]
+        ys = sb_ref[p, 1, rows, :]
+        zs = sb_ref[p, 2, rows, :]
+        area = sb_ref[p, 3, rows, :]
+        sj = sb_ref[p, 4, rows, :]
+        cj = sb_ref[p, 5, rows, :]
+        for h in range(halves):
+            lanes = pl.ds(h * LANES, LANES)
+            xt = tb_ref[g, 0, :, lanes]
+            yt = tb_ref[g, 1, :, lanes]
+            zt = tb_ref[g, 2, :, lanes]
+            et = tb_ref[g, 3, :, lanes]
+            zt4 = tb_ref[g, 4, :, lanes]
+            re, im = green(k, xt, yt, zt, zt4, et, xs, ys, zs, area, sj, cj)
             tr_ref[rows, lanes] = re.astype(jnp.bfloat16)
             ti_ref[rows, lanes] = im.astype(jnp.bfloat16)
-            return carry
-
-        lax.fori_loop(0, width // STRIP, strip, 0)
+        return carry
+
+    lax.fori_loop(0, width // STRIP, strip, 0, unroll=UNROLL)
 
 
 def entry_product(l_ref, p, tr, ti):
@@ -154,9 +156,16 @@
 
     target_geo = lax.dynamic_slice_in_dim(geometry, clus_index * cpd, cpd, axis=1)
     tq = jnp.stack(
-        [target_geo[0], target_geo[1], target_geo[2], jnp.exp(wavenum * target_geo[2])], axis=1
+        [
+            target_geo[0],
+            target_geo[1],
+            target_geo[2],
+            jnp.exp(wavenum * target_geo[2]),
+            4.0 * target_geo[2],
+        ],
+        axis=1,
     )
-    tb = jnp.broadcast_to(tq[:, :, None, :], (cpd, 4, STRIP, targets))
+    tb = jnp.broadcast_to(tq[:, :, None, :], (cpd, tq.shape[1], STRIP, targets))
 
     base_ids = jnp.arange(clus_count, dtype=jnp.int32)[:, None] * cpd
     source_ids = (base_ids + jnp.maximum(requests[0], 0)).reshape(-1)

time: 314 us -> 260 us (0.83); the launches traced: 310 us -> 260 us
  waiting for transfers between devices: 160 us -> 71.1 us
  Pallas kernels: 71.6 us -> 108 us
    reduce_scatter x2, waiting for transfers between devices: 149 us -> 60.4 us  [finish(): lax.psum_scatter(jnp.transpose(acc, (2, 0, 1)), ('src', 'sub'), scatter_d...]
    pallas_call x2, Pallas kernels: 71.6 us -> 108 us  [product(): pl.pallas_call(product_kernel, out_shape=jax.ShapeDtypeStruct((clusters,...]
  transfers between devices with their start and end apart: 4 -> 4, of which waited for: 3 -> 3; matrix products, arithmetic and copies ran while one was open for 4% -> 6% of each run, Pallas kernels for 0% -> 0%
where the time goes in v1:
time: 260 us
  Pallas kernels  108 us (42%)
  waiting for transfers between devices  71.1 us (27%)
  local copies, waits for them, and re-layouts  23.3 us (9%)
  blocking collectives  20 us (8%)
  between operations  14.9 us (6%)
  other arithmetic  11.5 us (4%)
  starting transfers between devices  10.5 us (4%)
    pallas_call x2, Pallas kernels, product(): pl.pallas_call(product_kernel, out_shape=jax.ShapeDtypeStruct((clusters,...  108 us
    reduce_scatter x2, waiting for transfers between devices, finish(): lax.psum_scatter(jnp.transpose(acc, (2, 0, 1)), ('src', 'sub'), scatter_d...  60.4 us
    all_to_all x1, blocking collectives, fetch(): lax.all_to_all(picked, 'clus', split_axis=1, concat_axis=1, tiled=True)  17.9 us
    all_to_all x1, waiting for transfers between devices, fetch(): lax.all_to_all(picked, 'clus', split_axis=1, concat_axis=1, tiled=True)  10.7 us
    transpose x2, local copies, waits for them, and re-layouts, finish(): jnp.transpose(acc, (2, 0, 1))  5.89 us
    unnamed x12, local copies, waits for them, and re-layouts  5.62 us
    all_to_all x1, starting transfers between devices, local(): lax.all_to_all(requests[0], 'clus', split_axis=0, concat_axis=0, tiled=True)  5.46 us
  transfers between devices with their start and end apart: 4, of which 3 were waited for; matrix products, arithmetic and copies ran while one was open for 6% of the time, Pallas kernels for 0%

profile of v1, /device:TPU:8, one launch (start us, length us, event | category | flops | bytes accessed | tf_op | source)
XLA Modules:
  0.0 259.7 jit_solution(2927041311380439853)
XLA Ops:
  7.2 5.5 %all-to-all-start = ((s32[4,1,4]{2,1,0:T(1,128)}), s32[4,1,4]{2,1,0:T(1,128)S(1)}, u32[]{:S(2)}, u32[]{:S(2)}) async-start(s32[4,1,4]{2,1,0:T(1,128)} %bitcast.83), calls=%async_computation | async-start | bytes 4096 | tf_op jit(solution)/shard_map/all_to_all | solution.py:139
  12.6 0.7 broadcast_maximum_fusion
  13.4 0.1 add.77
  13.4 0.1 add.81
  13.5 0.1 add.78
  13.6 0.1 max.27
  13.7 0.1 max.26
  13.8 0.7 copy.62
  14.5 0.7 iota_compare_fusion.1
  15.2 0.3 convert_reduce_fusion
  15.5 0.1 reshape.169
  15.5 0.6 convert_reduce_fusion.1
  16.2 3.2 %sort.17 = (s32[192]{0:T(256)}, s32[192]{0:T(256)S(1)}) sort(s32[192]{0:T(256)S(1)} %compare_convert_fusion.1, s32[192]{0:T(256)S(1)} %iota.22), dimensions={0}, to_apply=%region_2.3 | sort | flops 1536 | bytes 3072 | tf_op jit(solution)/shard_map/jit(argsort)/sort | solution.py:186
  20.0 1.6 gather_fusion.1
  21.6 0.8 constant_dynamic-update-slice_fusion.4
  22.4 0.7 constant_dynamic-update-slice_fusion.3
  23.1 0.7 constant_dynamic-update-slice_fusion.2
  23.8 0.7 constant_dynamic-update-slice_fusion.1
  24.6 0.8 constant_dynamic-update-slice_fusion
  25.4 1.6 gather_fusion
  27.0 0.6 fusion.4
  27.6 0.1 max.29
  27.7 0.1 fusion.1
  27.8 0.6 gather_fusion.2
  28.5 0.3 copy.50
  28.8 0.1 reshape.170
  28.9 0.9 bitcast_multiply_fusion.1
  29.8 5.0 %all-to-all-start.1 = ((bf16[128,16,128]{0,2,1:T(8,128)(2,1)}), bf16[128,16,128]{0,2,1:T(8,128)(2,1)S(1)}, u32[]{:S(2)}, u32[]{:S(2)}) async-start(bf16[128,16,128]{0,2,1:T(8,128)(2,1)} %bitcast_multiply_fusion.1), calls=%async_computation.1 | async-start | bytes 1048576 | tf_op jit(solution)/shard_map/all_to_all | solution.py:147
  34.9 10.7 %all-to-all-done.1 = bf16[128,16,128]{0,2,1:T(8,128)(2,1)S(1)} async-done(((bf16[128,16,128]{0,2,1:T(8,128)(2,1)}), bf16[128,16,128]{0,2,1:T(8,128)(2,1)S(1)}, u32[]{:S(2)}, u32[]{:S(2)}) %all-to-all-start.1) | async-done | bytes 524320 | tf_op jit(solution)/shard_map/all_to_all | solution.py:147
  45.7 0.1 pad_maximum_fusion
  45.8 1.1 copy.51.l_ref
  46.8 3.8 %broadcast_in_dim.49.sb_ref = f32[16,6,128,128]{3,2,1,0:T(8,128)} broadcast(f32[16,6,128]{2,1,0:T(8,128)S(1)} %copy.48), dimensions={0,1,2} | broadcast | bytes 6340608 | tf_op jit(solution)/shard_map/broadcast_in_dim | solution.py:177
  50.6 1.0 broadcast_in_dim.46.tb_ref
  51.7 54.3 %shard_map.80 = f32[12,128,256]{2,1,0:T(8,128)} custom-call(s32[1]{0:T(128)} %bitcast.1.n_ref, s32[192]{0:T(256)} %get-tuple-element.21.g_ref, s32[192]{0:T(256)} %get-tuple-element.20.p_ref, f32[192]{0:T(256)} %get-tuple-element.19.w_ref, f32[1]{0:T(128)} %copy.73.k_ref, f32[12,5,16,256]{3,2,1,0:T(8,128)} %broadcast_in_dim.46.tb_ref, ...), custom_call_target="tpu_custom_call" | custom-call | flops 3598712832 | bytes 12582912 | tf_op jit(solution)/shard_map/pallas_call | solution.py:112
  106.0 2.9 %copy.52 = f32[256,12,128]{2,1,0:T(8,128)} copy(f32[256,12,128]{0,2,1:T(8,128)} %bitcast.81) | data formatting | bytes 3145728 | tf_op jit(solution)/shard_map/transpose | solution.py:195
  109.0 30.6 %reduce-scatter.3.cloned.1.call-done = f32[64,12,128]{2,1,0:T(8,128)} async-done(((f32[256,12,128]{2,1,0:T(8,128)}), f32[64,12,128]{2,1,0:T(8,128)}) %reduce-scatter.3.cloned.1.call-update) | async-done | bytes 393232 | tf_op jit(solution)/shard_map/reduce_scatter | solution.py:194
  139.6 1.2 subtract_convert_fusion
  140.9 2.1 all_gather.3
  143.0 0.6 gather_fusion.3
  143.6 0.3 copy.54
  143.9 0.1 bitcast_multiply_fusion
  144.1 17.9 %all_to_all.19 = bf16[128,16,128]{0,2,1:T(8,128)(2,1)S(1)} all-to-all(bf16[128,16,128]{0,2,1:T(8,128)(2,1)S(1)} %bitcast_multiply_fusion), channel_id=1, replica_groups=mesh['freq'=2,'clus'=4,'src'=2,'sub'=2] {'clus'}, dimensions={1} | all-to-all | bytes 1048576 | tf_op jit(solution)/shard_map/all_to_all | solution.py:147
  162.1 1.2 pad_maximum_fusion.1.l_ref
  163.2 54.2 %shard_map.81 = f32[12,128,256]{2,1,0:T(8,128)} custom-call(s32[1]{0:T(128)} %bitcast.1.n_ref, s32[192]{0:T(256)} %get-tuple-element.21.g_ref, s32[192]{0:T(256)} %get-tuple-element.20.p_ref, f32[192]{0:T(256)} %get-tuple-element.19.w_ref, f32[1]{0:T(128)} %copy.73.k_ref, f32[12,5,16,256]{3,2,1,0:T(8,128)} %broadcast_in_dim.46.tb_ref, ...), custom_call_target="tpu_custom_call" | custom-call | flops 3598712832 | bytes 12582912 | tf_op jit(solution)/shard_map/pallas_call | solution.py:112
  217.4 3.0 %copy.56 = f32[256,12,128]{2,1,0:T(8,128)} copy(f32[256,12,128]{0,2,1:T(8,128)} %bitcast.80) | data formatting | bytes 3145728 | tf_op jit(solution)/shard_map/transpose | solution.py:195
  220.4 29.8 %reduce-scatter.5.cloned.1.call-done = f32[64,12,128]{2,1,0:T(8,128)} async-done(((f32[256,12,128]{2,1,0:T(8,128)}), f32[64,12,128]{2,1,0:T(8,128)}) %reduce-scatter.5.cloned.1.call-update) | async-done | bytes 393232 | tf_op jit(solution)/shard_map/reduce_scatter | solution.py:194
  250.2 1.9 copy.57
  252.1 0.7 copy.74
  (32 shorter events, 0.5 us)
Async XLA Ops:
  7.2 20.7 %copy-start = (bf16[128,12,128]{2,0,1:T(8,128)(2,1)S(1)}, bf16[128,12,128]{2,0,1:T(8,128)(2,1)}, u32[]{:S(2)}) copy-start(bf16[128,12,128]{2,0,1:T(8,128)(2,1)} %param.8) | copy-start | bytes 1179652
  7.2 20.4 %all-to-all-start = ((s32[4,1,4]{2,1,0:T(1,128)}), s32[4,1,4]{2,1,0:T(1,128)S(1)}, u32[]{:S(2)}, u32[]{:S(2)}) async-start(s32[4,1,4]{2,1,0:T(1,128)} %bitcast.83), calls=%async_computation | async-start | bytes 4096 | tf_op jit(solution)/shard_map/all_to_all | solution.py:139
  29.8 15.7 %all-to-all-start.1 = ((bf16[128,16,128]{0,2,1:T(8,128)(2,1)}), bf16[128,16,128]{0,2,1:T(8,128)(2,1)S(1)}, u32[]{:S(2)}, u32[]{:S(2)}) async-start(bf16[128,16,128]{0,2,1:T(8,128)(2,1)} %bitcast_multiply_fusion.1), calls=%async_computation.1 | async-start | bytes 1048576 | tf_op jit(solution)/shard_map/all_to_all | solution.py:147
  34.8 104.8 %reduce-scatter.3.cloned.1.call-start = ((), (), s32[]{:S(2)}) async-start(), calls=%async_computation.5 | async-start | bytes 2621440 | tf_op jit(solution)/shard_map/reduce_scatter | solution.py:194
  108.9 141.3 %reduce-scatter.5.cloned.1.call-start = ((), (), s32[]{:S(2)}) async-start(), calls=%async_computation.6 | async-start | bytes 2621440 | tf_op jit(solution)/shard_map/reduce_scatter | solution.py:194
Sparse Core Ops, SparseCore 0:
  109.0 30.5 reduce-scatter.2
  220.5 29.6 reduce-scatter.4
